TPU v7x, 256 devices: a whole 4x4x8 slice. The times are simulated.
256 devices in a mesh: dp: 32 (over y, z), mp: 8 (over x, core).
Axes of the slice: x: 4, y: 4, z: 8, core: 2. Of those that a mesh axis runs over, the one named last changes fastest.
Arguments:
- hidden: bfloat16 [512, 32, 1024], P(('dp', 'mp')), may hold values from -96 to 96, as said below
- query_weight: bfloat16 [1024, 1024], P('dp', 'mp'), may hold values from -0.1875 to 0.1875
- w_key: bfloat16 [1024, 1024], P('dp', 'mp'), may hold values from -0.1875 to 0.1875
- w_value: bfloat16 [1024, 1024], P('dp', 'mp'), may hold values from -0.1875 to 0.1875
- rel_table: bfloat16 [512, 1024], P('dp'), may hold values from -6 to 6
- rel_bucket: int32 [32, 32], replicated, may hold values from 0 to 511
- w_out: bfloat16 [1024, 1024], P('mp', 'dp'), may hold values from -0.1875 to 0.1875
- w_up: bfloat16 [1024, 4096], P('dp', 'mp'), may hold values from -0.1875 to 0.1875
- w_down: bfloat16 [4096, 1024], P('mp', 'dp'), may hold values from -0.09375 to 0.09375
- w_proj: bfloat16 [1024, 128], P(('dp', 'mp')), may hold values from -0.1875 to 0.1875
- pages: bfloat16 [8192, 128, 128], P('dp'), may hold values from -0.59765625 to 0.59765625
- page_len: int32 [8192], P('dp'), may hold values from 1 to 128
- slot_per_page: int32 [8192], replicated, may hold values from 0 to 8191, as said below
- candidates: int32 [512, 16, 4], P(('dp', 'mp')), may hold values from 0 to 8191, as said below
Outputs:
- query_vectors: bfloat16 [512, 32, 128], P(('dp', 'mp'))
- scores: float32 [512, 16], P(('dp', 'mp'))
Inputs may be any that keep to these rules, and one draw needn't show every extreme that they name: slot_per_page is a permutation of the slots; the page in slot s is held by index s // 256 of dp. `candidates`: among the 128 page ids of the 2 queries of one device (queries in aligned blocks of 2), at most 8 have slots held by any one index of dp, and in every such block some index of dp holds exactly 8 of them. `hidden`: token states are finite.
All inputs are finite; a program needn't handle non-finite values.
Results may differ from a plain program's by a relative error of at most 0.025.
Values may be sent and summed in bfloat16 or wider, within the bound.
No kernel may reach another device: no remote copies, remote signals or barrier semaphores. Data moves between devices by JAX's collectives and lax.ppermute only.
A program may use at most 64 MiB of HBM per device.

v0:
```python
import jax
import jax.numpy as jnp
from jax import lax
from jax.sharding import PartitionSpec as P

HD = 64


def layer_norm(value):
    mean = jnp.mean(value, axis=-1, keepdims=True)
    centered = value - mean
    var = jnp.mean(centered * centered, axis=-1, keepdims=True)
    return centered / jnp.sqrt(var + 1e-07)


def add_rows(left, piece):
    return jnp.dot(left, piece, preferred_element_type=jnp.float32)


def return_maxima(maxima):
    return lax.all_to_all(
        maxima.astype(jnp.bfloat16), "dp", split_axis=0, concat_axis=0, tiled=True
    ).astype(maxima.dtype)


def body(
    hidden,
    query_weight,
    w_key,
    w_value,
    rel_table,
    rel_bucket,
    w_out,
    w_up,
    w_down,
    w_proj,
    pages,
    page_len,
    slot_per_page,
    candidates,
):
    qry_dev, qlen, width = hidden.shape
    heads_local = query_weight.shape[1] // HD
    cols = query_weight.shape[1]
    tokens = lax.all_gather(hidden, "mp", axis=0, tiled=True)
    group = tokens.shape[0]
    flat = tokens.reshape(group * qlen, width)
    left_rel = lax.all_gather(rel_table, "dp", axis=0, tiled=True)
    pieces = (
        lax.all_gather(query_weight, "dp", axis=0, tiled=True),
        lax.all_gather(w_key, "dp", axis=0, tiled=True),
        lax.all_gather(w_value, "dp", axis=0, tiled=True),
    )
    qsum = add_rows(flat, pieces[0])
    ksum = add_rows(flat, pieces[1])
    vsum = add_rows(flat, pieces[2])
    qrsum = add_rows(left_rel, pieces[0])
    krsum = add_rows(left_rel, pieces[1])
    rel_q = qrsum.astype(jnp.bfloat16)
    rel_k = krsum.astype(jnp.bfloat16)
    nbuck = rel_q.shape[0]
    qx = qsum.astype(jnp.bfloat16).reshape(group, qlen, heads_local, HD)
    kx = ksum.astype(jnp.bfloat16).reshape(group, qlen, heads_local, HD)
    vx = vsum.astype(jnp.bfloat16).reshape(group, qlen, heads_local, HD)
    rel_q = rel_q.reshape(nbuck, heads_local, HD)
    rel_k = rel_k.reshape(nbuck, heads_local, HD)
    onehot = (rel_bucket[:, :, None] == jnp.arange(nbuck, dtype=jnp.int32)[None, None, :]).astype(
        jnp.float32
    )
    scale = 1.0 / jnp.sqrt(jnp.float32(3 * HD))
    content = jnp.einsum("qihd,qjhd->qhij", qx, kx, preferred_element_type=jnp.float32)
    along_axis_name = jnp.einsum("qihd,bhd->qhib", qx, rel_k, preferred_element_type=jnp.float32)
    c2p = jnp.einsum("qhib,ijb->qhij", along_axis_name, onehot, precision=lax.Precision.HIGHEST)
    back = jnp.einsum("qjhd,bhd->qhjb", kx, rel_q, preferred_element_type=jnp.float32)
    p2c = jnp.einsum("qhjb,jib->qhij", back, onehot, precision=lax.Precision.HIGHEST)
    logits = (content + c2p + p2c) * scale
    probs = jax.nn.softmax(logits, axis=-1).astype(jnp.bfloat16)
    context_rows = jnp.einsum("qhij,qjhd->qihd", probs, vx, preferred_element_type=jnp.float32)
    context_rows = context_rows.astype(jnp.bfloat16).reshape(group * qlen, cols)
    attn_terms = jnp.dot(
        context_rows,
        lax.all_gather(w_out, "dp", axis=1, tiled=True),
        preferred_element_type=jnp.float32,
    )
    attn = lax.psum_scatter(
        attn_terms.astype(jnp.bfloat16), "mp", scatter_dimension=0, tiled=True
    ).astype(jnp.float32)
    own = hidden.reshape(qry_dev * qlen, width).astype(jnp.float32)
    mid = layer_norm(own + attn).astype(jnp.bfloat16)
    mid_all = lax.all_gather(mid, "mp", axis=0, tiled=True)
    up = add_rows(mid_all, lax.all_gather(w_up, "dp", axis=0, tiled=True))
    inner = jax.nn.gelu(up, approximate=False).astype(jnp.bfloat16)
    down_terms = jnp.dot(
        inner, lax.all_gather(w_down, "dp", axis=1, tiled=True), preferred_element_type=jnp.float32
    )
    mlp = lax.psum_scatter(
        down_terms.astype(jnp.bfloat16), "mp", scatter_dimension=0, tiled=True
    ).astype(jnp.float32)
    state = layer_norm(mid.astype(jnp.float32) + mlp).astype(jnp.bfloat16)
    width_out = w_proj.shape[1]
    proj = add_rows(state, lax.all_gather(w_proj, ("dp", "mp"), axis=0, tiled=True))
    vectors = (proj / jnp.sqrt(jnp.sum(proj * proj, axis=-1, keepdims=True) + 1e-06)).astype(
        jnp.bfloat16
    )
    vectors = vectors.reshape(qry_dev, qlen, width_out)
    page_owners = lax.axis_size("dp")
    pg_dev = pages.shape[0]
    ptok = pages.shape[1]
    ncand, ppc = (candidates.shape[1], candidates.shape[2])
    req = qry_dev * ncand * ppc
    cap = 2 * req // page_owners
    slots = slot_per_page[candidates.reshape(req)]
    dest = slots // pg_dev
    local = slots % pg_dev
    query_of = jnp.arange(req, dtype=jnp.int32) // (ncand * ppc)
    member = (dest[:, None] == jnp.arange(page_owners, dtype=jnp.int32)[None, :]).astype(jnp.int32)
    place = jnp.sum((jnp.cumsum(member, axis=0) - 1) * member, axis=1)
    index = dest * cap + place
    codes = jnp.full((page_owners * cap,), -1, jnp.int32).at[index].set(query_of * pg_dev + local)
    codes = codes.reshape(page_owners, cap)
    token_positions = jnp.arange(ptok, dtype=jnp.int32)
    rows_out = (
        jnp.zeros((page_owners * cap, qlen, width_out), jnp.bfloat16)
        .at[index]
        .set(vectors[query_of])
    )
    rows_out = rows_out.reshape(page_owners, cap, qlen, width_out)
    where_local = lax.all_to_all(codes, "dp", split_axis=0, concat_axis=0, tiled=True) % pg_dev
    chosen = pages[where_local]
    lens = page_len[where_local]
    sim = jnp.einsum(
        "snie,snte->snit",
        lax.all_to_all(rows_out, "dp", split_axis=0, concat_axis=0, tiled=True),
        chosen,
        preferred_element_type=jnp.float32,
    )
    valid = token_positions[None, None, None, :] < lens[:, :, None, None]
    returned = return_maxima(jnp.max(jnp.where(valid, sim, -1e30), axis=-1))
    best = returned.reshape(page_owners * cap, qlen)[index]
    best = best.reshape(qry_dev, ncand, ppc, qlen)
    scores = jnp.sum(jnp.max(best, axis=2), axis=-1)
    return (vectors, scores)


def solution(mesh):
    in_specs = (
        P(("dp", "mp"), None, None),
        P("dp", "mp"),
        P("dp", "mp"),
        P("dp", "mp"),
        P("dp", None),
        P(),
        P("mp", "dp"),
        P("dp", "mp"),
        P("mp", "dp"),
        P(("dp", "mp"), None),
        P("dp", None, None),
        P("dp"),
        P(),
        P(("dp", "mp"), None, None),
    )
    out_specs = (P(("dp", "mp"), None, None), P(("dp", "mp"), None))
    return jax.shard_map(body, mesh=mesh, in_specs=in_specs, out_specs=out_specs, check_vma=False)
```

profile of v0, /device:TPU:1, one launch (start us, length us, event | category | flops | bytes accessed | tf_op | source)
XLA Modules:
  0.0 620.8 jit_solution(7747046523202727993)
XLA Ops:
  7.2 0.7 all-gather.7.cloned.1.call-update
  8.0 0.7 all-gather.9.cloned.1.call-update
  8.7 41.4 %all_gather.32 = bf16[1024,128]{1,0:T(8,128)(2,1)S(1)} all-gather(bf16[32,128]{1,0:T(8,128)(2,1)} %param.15), channel_id=1, replica_groups=mesh['dp'=32,'mp'=8] {'dp'}, dimensions={0}, use_global_device_ids=true | all-gather | bytes 270336 | tf_op jit(solution)/shard_map/all_gather | solution.py:50
  50.1 38.1 %all_gather.33 = bf16[1024,128]{1,0:T(8,128)(2,1)S(1)} all-gather(bf16[32,128]{1,0:T(8,128)(2,1)} %param.16), channel_id=1, replica_groups=mesh['dp'=32,'mp'=8] {'dp'}, dimensions={0}, use_global_device_ids=true | all-gather | bytes 270336 | tf_op jit(solution)/shard_map/all_gather | solution.py:51
  88.1 37.2 %all_gather.31 = bf16[1024,128]{1,0:T(8,128)(2,1)S(1)} all-gather(bf16[32,128]{1,0:T(8,128)(2,1)} %param.17), channel_id=1, replica_groups=mesh['dp'=32,'mp'=8] {'dp'}, dimensions={0}, use_global_device_ids=true | all-gather | bytes 270336 | tf_op jit(solution)/shard_map/all_gather | solution.py:52
  125.3 35.7 %all_gather.35 = bf16[128,1024]{0,1:T(8,128)(2,1)S(1)} all-gather(bf16[128,32]{0,1:T(8,128)(2,1)} %param.20), channel_id=1, replica_groups=mesh['dp'=32,'mp'=8] {'dp'}, dimensions={1}, use_global_device_ids=true | all-gather | bytes 270336 | tf_op jit(solution)/shard_map/all_gather | solution.py:82
  161.0 1.7 convolution_convert_fusion.6
  162.9 1.7 convolution_convert_fusion.5
  164.7 0.4 convolution_convert_fusion.7
  165.3 1.7 convolution_convert_fusion.4
  167.1 0.5 fusion.59
  167.6 1.4 fusion.3
  169.3 0.5 convolution_convert_fusion.3
  169.8 0.5 fusion.57
  170.2 1.4 fusion.1
  171.7 0.5 fusion.11
  173.0 1.4 convolution_convert_fusion
  174.5 0.5 all-gather.13.cloned.1.call-update
  175.1 0.5 all-gather.15.cloned.1.call-update
  175.7 73.5 %reduce-scatter.3.cloned.1.call-done = bf16[64,1024]{1,0:T(8,128)(2,1)} async-done(((bf16[512,1024]{1,0:T(8,128)(2,1)}), bf16[64,1024]{1,0:T(8,128)(2,1)}) %reduce-scatter.3.cloned.1.call-update) | async-done | bytes 131088 | tf_op jit(solution)/shard_map/reduce_scatter | solution.py:85
  249.2 1.0 fusion.67
  250.3 1.1 multiply_reduce_fusion.1
  251.4 1.7 divide_convert_fusion.3
  253.4 70.8 %all-gather.13.cloned.1.call-done = bf16[1024,512]{1,0:T(8,128)(2,1)} async-done(((bf16[32,512]{1,0:T(8,128)(2,1)}), bf16[1024,512]{1,0:T(8,128)(2,1)}) %all-gather.13.cloned.1.call-update) | async-done | bytes 1048592 | tf_op jit(solution)/shard_map/all_gather | solution.py:91
  324.1 76.3 %all-gather.15.cloned.1.call-done = bf16[512,1024]{0,1:T(8,128)(2,1)} async-done(((bf16[512,32]{0,1:T(8,128)(2,1)}), bf16[512,1024]{0,1:T(8,128)(2,1)}) %all-gather.15.cloned.1.call-update) | async-done | bytes 1048592 | tf_op jit(solution)/shard_map/all_gather | solution.py:94
  400.4 30.5 %all-gather.11.cloned.1.call-done = bf16[512,1024]{1,0:T(8,128)(2,1)} async-done(((bf16[64,1024]{1,0:T(8,128)(2,1)}), bf16[512,1024]{1,0:T(8,128)(2,1)}) %all-gather.11.cloned.1.call-update) | async-done | bytes 1048592 | tf_op jit(solution)/shard_map/all_gather | solution.py:90
  430.9 6.2 %convolution_convert_fusion.1 = bf16[512,1024]{1,0:T(8,128)(2,1)} fusion(bf16[512,1024]{0,1:T(8,128)(2,1)} %all-gather.15.cloned.1.call-done, bf16[512,1024]{1,0:T(8,128)(2,1)} %all-gather.11.cloned.1.call-done, bf16[1024,512]{1,0:T(8,128)(2,1)} %all-gather.13.cloned.1.call-done), kind=kOutput, calls=%fused_computation.17 | convolution fusion | flops 1091305472 | bytes 4194304 | tf_op jit(solution)/shard_map/dot_general | solution.py:93
  437.4 1.1 gather_fusion
  439.0 1.0 scatter_custom_fusion
  440.0 0.7 all_to_all.14
  440.7 9.6 %all-to-all-start = ((s32[32,1,8]{2,1,0:T(1,128)}), s32[32,1,8]{2,1,0:T(1,128)S(1)}, u32[]{:S(2)}, u32[]{:S(2)}) async-start(s32[32,1,8]{2,1,0:T(1,128)} %bitcast.21), calls=%async_computation.2 | async-start | bytes 32768 | tf_op jit(solution)/shard_map/all_to_all | solution.py:128
  450.3 62.5 %all-gather = bf16[256,4,128]{2,1,0:T(4,128)(2,1)S(1)} all-gather(bf16[1,4,128]{2,1,0:T(4,128)(2,1)S(1)} %bitcast.96), channel_id=1, replica_groups=mesh['dp'=32,'mp'=8] {'dp','mp'}, dimensions={0}, use_global_device_ids=true | all-gather | bytes 263168 | tf_op jit(solution)/shard_map/all_gather | solution.py:101
  512.8 1.0 fusion.65
  513.9 1.1 multiply_reduce_fusion
  515.0 1.3 multiply_reduce_fusion.2
  516.4 0.8 gather_fusion.2
  517.2 1.7 broadcast_in_dim.14
  518.8 13.7 %scatter_fusion = bf16[256,32,128]{2,1,0:T(8,128)(2,1)} fusion(bf16[256,32,128]{2,1,0:T(8,128)(2,1)} %broadcast_in_dim.14, s32[128]{0:T(128)S(1)} %fusion.75, bf16[128,32,128]{2,1,0:T(8,128)(2,1)S(1)} %gather_fusion.2), kind=kCustom, calls=%fused_computation.6 | custom fusion | bytes 3146240 | tf_op jit(solution)/shard_map/scatter | solution.py:125
  532.5 6.3 %all-to-all-start.1 = ((bf16[32,8,32,128]{3,2,1,0:T(8,128)(2,1)}), bf16[32,8,32,128]{3,2,1,0:T(8,128)(2,1)S(1)}, u32[]{:S(2)}, u32[]{:S(2)}) async-start(bf16[32,8,32,128]{3,2,1,0:T(8,128)(2,1)} %bitcast.24), calls=%async_computation.3 | async-start | bytes 4194304 | tf_op jit(solution)/shard_map/all_to_all | solution.py:133
  538.9 11.8 %gather_fusion.3 = bf16[256,128,128]{2,1,0:T(8,128)(2,1)} fusion(bf16[256,128,128]{2,1,0:T(8,128)(2,1)} %param.24, s32[1024]{0:T(1024)S(1)} %pad_clamp_fusion.2), kind=kCustom, calls=%fused_computation.3 | custom fusion | bytes 16778240 | tf_op jit(solution)/shard_map/gather | solution.py:129
  550.8 1.9 gather_fusion.1
  552.9 34.5 %all-to-all-done.1 = bf16[32,8,32,128]{3,2,1,0:T(8,128)(2,1)S(1)} async-done(((bf16[32,8,32,128]{3,2,1,0:T(8,128)(2,1)}), bf16[32,8,32,128]{3,2,1,0:T(8,128)(2,1)S(1)}, u32[]{:S(2)}, u32[]{:S(2)}) %all-to-all-start.1) | async-done | bytes 2097184 | tf_op jit(solution)/shard_map/all_to_all | solution.py:133
  587.4 8.0 %select_reduce_fusion = bf16[32,8,32]{2,1,0:T(8,128)(2,1)S(1)} fusion(bf16[32,8,32,128]{3,2,1,0:T(8,128)(2,1)S(1)} %all-to-all-done.1, bf16[32,8,128,128]{3,2,1,0:T(8,128)(2,1)} %bitcast.87, pred[32,8,128]{2,1,0:T(8,128)(4,1)S(1)} %iota_compare_fusion.1), kind=kOutput, calls=%fused_computation.8 | convolution fusion | flops 270524416 | bytes 10534912 | tf_op jit(solution)/shard_map/snie,snte->snit/dot_general | solution.py:131
  595.3 0.7 reshape.374
  596.0 7.8 %all-to-all-start.2 = ((bf16[32,2,128]{2,1,0:T(2,128)(2,1)}), bf16[32,2,128]{2,1,0:T(2,128)(2,1)S(1)}, u32[]{:S(2)}, u32[]{:S(2)}) async-start(bf16[32,2,128]{2,1,0:T(2,128)(2,1)} %reshape.374), calls=%async_computation.4 | async-start | bytes 32768 | tf_op jit(solution)/shard_map/all_to_all | solution.py:21
  603.8 8.6 %all-to-all-done.2 = bf16[32,2,128]{2,1,0:T(2,128)(2,1)S(1)} async-done(((bf16[32,2,128]{2,1,0:T(2,128)(2,1)}), bf16[32,2,128]{2,1,0:T(2,128)(2,1)S(1)}, u32[]{:S(2)}, u32[]{:S(2)}) %all-to-all-start.2) | async-done | bytes 16416 | tf_op jit(solution)/shard_map/all_to_all | solution.py:21
  612.6 0.6 gather_fusion.4
  613.3 0.7 reduce_sum.82
  (68 shorter events, 3.4 us)
Async XLA Ops:
  7.2 430.2 %copy-start = (s32[8192]{0:T(1024)S(1)}, s32[8192]{0:T(1024)}, u32[]{:S(2)}) copy-start(s32[8192]{0:T(1024)} %param.26) | copy-start | bytes 98308
  7.2 153.8 %all-gather.7.cloned.1.call-start = ((), (), s32[]{:S(2)}) async-start(), calls=%async_computation.5 | async-start | bytes 1179648 | tf_op jit(solution)/shard_map/all_gather | solution.py:45
  7.9 157.4 %all-gather.9.cloned.1.call-start = ((), (), s32[]{:S(2)}) async-start(), calls=%async_computation.6 | async-start | bytes 1081344 | tf_op jit(solution)/shard_map/all_gather | solution.py:48
  8.7 240.6 %reduce-scatter.3.cloned.1.call-start = ((), (), s32[]{:S(2)}) async-start(), calls=%async_computation.7 | async-start | bytes 1179648 | tf_op jit(solution)/shard_map/reduce_scatter | solution.py:85
  161.0 3.7 copy-start.3
  165.2 2.4 copy-start.7
  167.5 1.7 copy-start.4
  172.6 76.6 %copy-start.5 = (bf16[2,32,1024]{2,1,0:T(8,128)(2,1)S(1)}, bf16[2,32,1024]{2,1,0:T(8,128)(2,1)}, u32[]{:S(2)}) copy-start(bf16[2,32,1024]{2,1,0:T(8,128)(2,1)} %param.14) | copy-start | bytes 393220
  174.5 149.6 %all-gather.13.cloned.1.call-start = ((), (), s32[]{:S(2)}) async-start(), calls=%async_computation.9 | async-start | bytes 1081344 | tf_op jit(solution)/shard_map/all_gather | solution.py:91
  175.1 225.4 %all-gather.15.cloned.1.call-start = ((), (), s32[]{:S(2)}) async-start(), calls=%async_computation.10 | async-start | bytes 1081344 | tf_op jit(solution)/shard_map/all_gather | solution.py:94
  175.7 255.2 %all-gather.11.cloned.1.call-start = ((), (), s32[]{:S(2)}) async-start(), calls=%async_computation.8 | async-start | bytes 1179648 | tf_op jit(solution)/shard_map/all_gather | solution.py:90
  253.1 184.0 %copy-start.8 = (s32[2,16,4]{1,2,0:T(4,128)S(1)}, s32[2,16,4]{1,2,0:T(4,128)}, u32[]{:S(2)}) copy-start(s32[2,16,4]{1,2,0:T(4,128)} %param.27) | copy-start | bytes 1540
  253.1 197.2 %copy-start.9 = (bf16[4,128]{1,0:T(4,128)(2,1)S(1)}, bf16[4,128]{1,0:T(4,128)(2,1)}, u32[]{:S(2)}) copy-start(bf16[4,128]{1,0:T(4,128)(2,1)} %param.23) | copy-start | bytes 3076
  253.1 259.7 %reduce-scatter.5.cloned.1.call-start = ((), (), s32[]{:S(2)}) async-start(), calls=%async_computation.11 | async-start | bytes 1179648 | tf_op jit(solution)/shard_map/reduce_scatter | solution.py:96
  437.1 75.7 %copy-start.6 = (bf16[64,1024]{1,0:T(8,128)(2,1)S(1)}, bf16[64,1024]{1,0:T(8,128)(2,1)}, u32[]{:S(2)}) copy-start(bf16[64,1024]{1,0:T(8,128)(2,1)} %divide_convert_fusion.3) | copy-start | bytes 393220
  440.7 91.9 %all-to-all-start = ((s32[32,1,8]{2,1,0:T(1,128)}), s32[32,1,8]{2,1,0:T(1,128)S(1)}, u32[]{:S(2)}, u32[]{:S(2)}) async-start(s32[32,1,8]{2,1,0:T(1,128)} %bitcast.21), calls=%async_computation.2 | async-start | bytes 32768 | tf_op jit(solution)/shard_map/all_to_all | solution.py:128
  516.4 2.5 copy-start.2
  532.5 54.9 %all-to-all-start.1 = ((bf16[32,8,32,128]{3,2,1,0:T(8,128)(2,1)}), bf16[32,8,32,128]{3,2,1,0:T(8,128)(2,1)S(1)}, u32[]{:S(2)}, u32[]{:S(2)}) async-start(bf16[32,8,32,128]{3,2,1,0:T(8,128)(2,1)} %bitcast.24), calls=%async_computation.3 | async-start | bytes 4194304 | tf_op jit(solution)/shard_map/all_to_all | solution.py:133
  538.9 11.8 %copy-start.1 = (s32[256]{0:T(256)S(1)}, s32[256]{0:T(256)}, u32[]{:S(2)}) copy-start(s32[256]{0:T(256)} %param.25) | copy-start | bytes 3076
  596.0 16.4 %all-to-all-start.2 = ((bf16[32,2,128]{2,1,0:T(2,128)(2,1)}), bf16[32,2,128]{2,1,0:T(2,128)(2,1)S(1)}, u32[]{:S(2)}, u32[]{:S(2)}) async-start(bf16[32,2,128]{2,1,0:T(2,128)(2,1)} %reshape.374), calls=%async_computation.4 | async-start | bytes 32768 | tf_op jit(solution)/shard_map/all_to_all | solution.py:21
Sparse Core Ops, SparseCore 0:
  9.8 29.9 all-gather.6
  42.4 71.3 all-gather.8
  174.6 74.5 reduce-scatter.2
  251.7 72.3 all-gather.12
  326.6 73.8 all-gather.14
  402.1 28.6 all-gather.10
  437.2 32.1 reduce-scatter.4
where the time goes:
time: 622 us; the launch traced here: 621 us
  waiting for transfers between devices  297 us (48%)
  blocking collectives  215 us (35%)
  local copies, waits for them, and re-layouts  35.7 us (6%)
  matrix products  27.4 us (4%)
  starting transfers between devices  24 us (4%)
  between operations  14.6 us (2%)
  other arithmetic  7.57 us (1%)
    all_gather x1, waiting for transfers between devices, body(): lax.all_gather(w_down, 'dp', axis=1, tiled=True)  76.3 us
    reduce_scatter x1, waiting for transfers between devices, body(): lax.psum_scatter(attn_terms.astype(jnp.bfloat16), 'mp', scatter_dimension...  73.5 us
    all_gather x1, waiting for transfers between devices, body(): up = add_rows(mid_all, lax.all_gather(w_up, 'dp', axis=0, tiled=True))  70.8 us
    all_gather x1, blocking collectives, body(): lax.all_gather(w_proj, ('dp', 'mp'), axis=0, tiled=True)  62.5 us
    all_gather x1, blocking collectives, body(): lax.all_gather(query_weight, 'dp', axis=0, tiled=True)  41.4 us
    all_gather x1, blocking collectives, body(): lax.all_gather(w_key, 'dp', axis=0, tiled=True)  38.1 us
    all_gather x1, blocking collectives, body(): lax.all_gather(w_value, 'dp', axis=0, tiled=True)  37.2 us
    all_gather x1, blocking collectives, body(): lax.all_gather(w_out, 'dp', axis=1, tiled=True)  35.7 us
  transfers between devices with their start and end apart: 10, of which 6 were waited for; matrix products, arithmetic and copies ran while one was open for 7% of the time, Pallas kernels for 0%

commit v1 on v0

--- a/solution.py
+++ b/solution.py
@@ -87,7 +87,24 @@
     ).astype(jnp.float32)
     own = hidden.reshape(qry_dev * qlen, width).astype(jnp.float32)
     mid = layer_norm(own + attn).astype(jnp.bfloat16)
-    mid_all = lax.all_gather(mid, "mp", axis=0, tiled=True)
+    length, position, extent = (lax.axis_size("mp"), lax.axis_index("mp"), mid.shape[0])
+    right = [(i, (i + 1) % length) for i in range(length)]
+    left_2 = [(i, (i - 1) % length) for i in range(length)]
+    out = jnp.zeros((*mid.shape[:0], length * extent, *mid.shape[0 + 1 :]), mid.dtype)
+    out = lax.dynamic_update_slice_in_dim(out, mid, position * extent, axis=0)
+    from_left = from_right = mid
+    half = length // 2
+    for step in range(1, half + 1):
+        from_left = lax.ppermute(from_left, "mp", right)
+        out = lax.dynamic_update_slice_in_dim(
+            out, from_left, (position - step) % length * extent, axis=0
+        )
+        if step < length - half:
+            from_right = lax.ppermute(from_right, "mp", left_2)
+            out = lax.dynamic_update_slice_in_dim(
+                out, from_right, (position + step) % length * extent, axis=0
+            )
+    mid_all = out
     up = add_rows(mid_all, lax.all_gather(w_up, "dp", axis=0, tiled=True))
     inner = jax.nn.gelu(up, approximate=False).astype(jnp.bfloat16)
     down_terms = jnp.dot(

time: 622 us -> 595 us (0.957)
  waiting for transfers between devices: 297 us -> 254 us
  starting transfers between devices: 24 us -> 33.7 us
    all_gather x1 -> x0, waiting for transfers between devices: 30.5 us -> none  [body(): mid_all = lax.all_gather(mid, 'mp', axis=0, tiled=True)]
    all_gather x1, waiting for transfers between devices: 70.8 us -> 50.9 us  [body(): up = add_rows(mid_all, lax.all_gather(w_up, 'dp', axis=0, tiled=True))]
    ppermute x0 -> x7, starting transfers between devices: none -> 12.5 us  [the longest x3 9.5 us: body(): from_right = lax.ppermute(from_right, 'mp', left_2)]
    ppermute x0 -> x7, waiting for transfers between devices: none -> 7.98 us  [the longest x4 7.84 us: body(): from_left = lax.ppermute(from_left, 'mp', right)]
  transfers between devices with their start and end apart: 10 -> 16, of which waited for: 6 -> 10; matrix products, arithmetic and copies ran while one was open for 7% -> 8% of each run, Pallas kernels for 0% -> 0%
where the time goes in v1:
time: 595 us; the launch traced here: 594 us
  waiting for transfers between devices  254 us (43%)
  blocking collectives  221 us (37%)
  local copies, waits for them, and re-layouts  36.6 us (6%)
  starting transfers between devices  33.7 us (6%)
  matrix products  27.1 us (5%)
  between operations  14.6 us (2%)
  other arithmetic  6.92 us (1%)
    all_gather x1, waiting for transfers between devices, body(): lax.all_gather(w_down, 'dp', axis=1, tiled=True)  76.3 us
    reduce_scatter x1, waiting for transfers between devices, body(): lax.psum_scatter(attn_terms.astype(jnp.bfloat16), 'mp', scatter_dimension...  73.3 us
    all_gather x1, blocking collectives, body(): lax.all_gather(w_proj, ('dp', 'mp'), axis=0, tiled=True)  68.6 us
    all_gather x1, waiting for transfers between devices, body(): up = add_rows(mid_all, lax.all_gather(w_up, 'dp', axis=0, tiled=True))  50.9 us
    all_gather x1, blocking collectives, body(): lax.all_gather(query_weight, 'dp', axis=0, tiled=True)  41.4 us
    all_gather x1, blocking collectives, body(): lax.all_gather(w_key, 'dp', axis=0, tiled=True)  38.1 us
    all_gather x1, blocking collectives, body(): lax.all_gather(w_value, 'dp', axis=0, tiled=True)  37.2 us
    all_gather x1, blocking collectives, body(): lax.all_gather(w_out, 'dp', axis=1, tiled=True)  35.6 us
  transfers between devices with their start and end apart: 16, of which 10 were waited for; matrix products, arithmetic and copies ran while one was open for 8% of the time, Pallas kernels for 0%

profile of v1, /device:TPU:1, one launch (start us, length us, event | category | flops | bytes accessed | tf_op | source)
XLA Modules:
  0.0 593.9 jit_solution(11726428633923320065)
XLA Ops:
  7.2 0.7 all-gather.6.cloned.1.call-update
  8.0 0.7 all-gather.8.cloned.1.call-update
  8.7 41.4 %all_gather.29 = bf16[1024,128]{1,0:T(8,128)(2,1)S(1)} all-gather(bf16[32,128]{1,0:T(8,128)(2,1)} %param.15), channel_id=1, replica_groups=mesh['dp'=32,'mp'=8] {'dp'}, dimensions={0}, use_global_device_ids=true | all-gather | bytes 270336 | tf_op jit(solution)/shard_map/all_gather | solution.py:50
  50.1 38.1 %all_gather.30 = bf16[1024,128]{1,0:T(8,128)(2,1)S(1)} all-gather(bf16[32,128]{1,0:T(8,128)(2,1)} %param.16), channel_id=1, replica_groups=mesh['dp'=32,'mp'=8] {'dp'}, dimensions={0}, use_global_device_ids=true | all-gather | bytes 270336 | tf_op jit(solution)/shard_map/all_gather | solution.py:51
  88.1 37.2 %all_gather.28 = bf16[1024,128]{1,0:T(8,128)(2,1)S(1)} all-gather(bf16[32,128]{1,0:T(8,128)(2,1)} %param.17), channel_id=1, replica_groups=mesh['dp'=32,'mp'=8] {'dp'}, dimensions={0}, use_global_device_ids=true | all-gather | bytes 270336 | tf_op jit(solution)/shard_map/all_gather | solution.py:52
  125.3 35.6 %all_gather.32 = bf16[128,1024]{0,1:T(8,128)(2,1)S(1)} all-gather(bf16[128,32]{0,1:T(8,128)(2,1)} %param.20), channel_id=1, replica_groups=mesh['dp'=32,'mp'=8] {'dp'}, dimensions={1}, use_global_device_ids=true | all-gather | bytes 270336 | tf_op jit(solution)/shard_map/all_gather | solution.py:82
  160.9 1.7 convolution_convert_fusion.6
  162.8 1.7 convolution_convert_fusion.5
  165.1 0.9 reshape.294
  166.0 1.7 convolution_convert_fusion.4
  168.2 1.4 fusion.3
  170.9 1.4 fusion.1
  173.7 1.4 convolution_convert_fusion
  176.5 73.3 %reduce-scatter.3.cloned.1.call-done = bf16[64,1024]{1,0:T(8,128)(2,1)} async-done(((bf16[512,1024]{1,0:T(8,128)(2,1)}), bf16[64,1024]{1,0:T(8,128)(2,1)}) %reduce-scatter.3.cloned.1.call-update) | async-done | bytes 131088 | tf_op jit(solution)/shard_map/reduce_scatter | solution.py:85
  249.8 1.0 fusion.67
  250.9 1.1 multiply_reduce_fusion.1
  252.1 1.0 constant_dynamic-update-slice_fusion.7
  253.2 1.0 collective-permute-start
  254.2 2.0 collective-permute-start.1
  256.1 0.8 collective-permute-done
  256.9 1.6 collective-permute-start.2
  258.6 3.2 collective-permute-start.3
  261.8 0.8 collective-permute-done.2
  262.9 4.4 collective-permute-start.5
  267.4 0.8 collective-permute-done.4
  268.3 5.4 collective-permute-done.6
  273.8 50.9 %all-gather.10.cloned.1.call-done = bf16[1024,512]{1,0:T(8,128)(2,1)} async-done(((bf16[32,512]{1,0:T(8,128)(2,1)}), bf16[1024,512]{1,0:T(8,128)(2,1)}) %all-gather.10.cloned.1.call-update) | async-done | bytes 1048592 | tf_op jit(solution)/shard_map/all_gather | solution.py:108
  324.7 76.3 %all-gather.12.cloned.1.call-done = bf16[512,1024]{0,1:T(8,128)(2,1)} async-done(((bf16[512,32]{0,1:T(8,128)(2,1)}), bf16[512,1024]{0,1:T(8,128)(2,1)}) %all-gather.12.cloned.1.call-update) | async-done | bytes 1048592 | tf_op jit(solution)/shard_map/all_gather | solution.py:111
  401.1 5.9 convolution_convert_fusion.1
  407.2 1.1 gather_fusion
  408.9 1.0 scatter_custom_fusion
  409.8 0.7 all_to_all.14
  410.5 6.0 %all-to-all-start = ((s32[32,1,8]{2,1,0:T(1,128)}), s32[32,1,8]{2,1,0:T(1,128)S(1)}, u32[]{:S(2)}, u32[]{:S(2)}) async-start(s32[32,1,8]{2,1,0:T(1,128)} %bitcast.21), calls=%async_computation.2 | async-start | bytes 32768 | tf_op jit(solution)/shard_map/all_to_all | solution.py:145
  416.6 68.6 %all-gather = bf16[256,4,128]{2,1,0:T(4,128)(2,1)S(1)} all-gather(bf16[1,4,128]{2,1,0:T(4,128)(2,1)S(1)} %bitcast.96), channel_id=1, replica_groups=mesh['dp'=32,'mp'=8] {'dp','mp'}, dimensions={0}, use_global_device_ids=true | all-gather | bytes 263168 | tf_op jit(solution)/shard_map/all_gather | solution.py:118
  485.2 1.0 fusion.65
  486.3 1.1 multiply_reduce_fusion
  487.4 1.3 multiply_reduce_fusion.2
  488.8 0.8 gather_fusion.2
  489.6 1.7 broadcast_in_dim.17
  491.2 13.7 %scatter_fusion = bf16[256,32,128]{2,1,0:T(8,128)(2,1)} fusion(bf16[256,32,128]{2,1,0:T(8,128)(2,1)} %broadcast_in_dim.17, s32[128]{0:T(128)S(1)} %fusion.75, bf16[128,32,128]{2,1,0:T(8,128)(2,1)S(1)} %gather_fusion.2), kind=kCustom, calls=%fused_computation.6 | custom fusion | bytes 3146240 | tf_op jit(solution)/shard_map/scatter | solution.py:142
  504.9 6.9 %all-to-all-start.1 = ((bf16[32,8,32,128]{3,2,1,0:T(8,128)(2,1)}), bf16[32,8,32,128]{3,2,1,0:T(8,128)(2,1)S(1)}, u32[]{:S(2)}, u32[]{:S(2)}) async-start(bf16[32,8,32,128]{3,2,1,0:T(8,128)(2,1)} %bitcast.24), calls=%async_computation.3 | async-start | bytes 4194304 | tf_op jit(solution)/shard_map/all_to_all | solution.py:150
  512.0 11.8 %gather_fusion.3 = bf16[256,128,128]{2,1,0:T(8,128)(2,1)} fusion(bf16[256,128,128]{2,1,0:T(8,128)(2,1)} %param.24, s32[1024]{0:T(1024)S(1)} %pad_clamp_fusion.2), kind=kCustom, calls=%fused_computation.3 | custom fusion | bytes 16778240 | tf_op jit(solution)/shard_map/gather | solution.py:146
  523.9 1.9 gather_fusion.1
  526.0 34.5 %all-to-all-done.1 = bf16[32,8,32,128]{3,2,1,0:T(8,128)(2,1)S(1)} async-done(((bf16[32,8,32,128]{3,2,1,0:T(8,128)(2,1)}), bf16[32,8,32,128]{3,2,1,0:T(8,128)(2,1)S(1)}, u32[]{:S(2)}, u32[]{:S(2)}) %all-to-all-start.1) | async-done | bytes 2097184 | tf_op jit(solution)/shard_map/all_to_all | solution.py:150
  560.5 8.0 %select_reduce_fusion = bf16[32,8,32]{2,1,0:T(8,128)(2,1)S(1)} fusion(bf16[32,8,32,128]{3,2,1,0:T(8,128)(2,1)S(1)} %all-to-all-done.1, bf16[32,8,128,128]{3,2,1,0:T(8,128)(2,1)} %bitcast.87, pred[32,8,128]{2,1,0:T(8,128)(4,1)S(1)} %iota_compare_fusion.1), kind=kOutput, calls=%fused_computation.8 | convolution fusion | flops 270524416 | bytes 10534912 | tf_op jit(solution)/shard_map/snie,snte->snit/dot_general | solution.py:148
  568.4 0.7 reshape.374
  569.1 7.8 %all-to-all-start.2 = ((bf16[32,2,128]{2,1,0:T(2,128)(2,1)}), bf16[32,2,128]{2,1,0:T(2,128)(2,1)S(1)}, u32[]{:S(2)}, u32[]{:S(2)}) async-start(bf16[32,2,128]{2,1,0:T(2,128)(2,1)} %reshape.374), calls=%async_computation.4 | async-start | bytes 32768 | tf_op jit(solution)/shard_map/all_to_all | solution.py:21
  576.9 8.6 %all-to-all-done.2 = bf16[32,2,128]{2,1,0:T(2,128)(2,1)S(1)} async-done(((bf16[32,2,128]{2,1,0:T(2,128)(2,1)}), bf16[32,2,128]{2,1,0:T(2,128)(2,1)S(1)}, u32[]{:S(2)}, u32[]{:S(2)}) %all-to-all-start.2) | async-done | bytes 16416 | tf_op jit(solution)/shard_map/all_to_all | solution.py:21
  (86 shorter events, 8.7 us)
Async XLA Ops:
  7.2 400.1 %copy-start = (s32[8192]{0:T(1024)S(1)}, s32[8192]{0:T(1024)}, u32[]{:S(2)}) copy-start(s32[8192]{0:T(1024)} %param.26) | copy-start | bytes 98308
  7.2 153.8 %all-gather.6.cloned.1.call-start = ((), (), s32[]{:S(2)}) async-start(), calls=%async_computation.5 | async-start | bytes 1179648 | tf_op jit(solution)/shard_map/all_gather | solution.py:45
  7.9 158.1 %all-gather.8.cloned.1.call-start = ((), (), s32[]{:S(2)}) async-start(), calls=%async_computation.6 | async-start | bytes 1081344 | tf_op jit(solution)/shard_map/all_gather | solution.py:48
  8.7 241.2 %reduce-scatter.3.cloned.1.call-start = ((), (), s32[]{:S(2)}) async-start(), calls=%async_computation.7 | async-start | bytes 1179648 | tf_op jit(solution)/shard_map/reduce_scatter | solution.py:85
  160.9 3.7 copy-start.3
  165.1 3.1 copy-start.7
  168.2 1.7 copy-start.4
  170.9 2.1 copy-start.6
  173.3 76.6 %copy-start.5 = (bf16[2,32,1024]{2,1,0:T(8,128)(2,1)S(1)}, bf16[2,32,1024]{2,1,0:T(8,128)(2,1)}, u32[]{:S(2)}) copy-start(bf16[2,32,1024]{2,1,0:T(8,128)(2,1)} %param.14) | copy-start | bytes 393220
  175.1 149.6 %all-gather.10.cloned.1.call-start = ((), (), s32[]{:S(2)}) async-start(), calls=%async_computation.8 | async-start | bytes 1081344 | tf_op jit(solution)/shard_map/all_gather | solution.py:108
  175.7 225.3 %all-gather.12.cloned.1.call-start = ((), (), s32[]{:S(2)}) async-start(), calls=%async_computation.9 | async-start | bytes 1081344 | tf_op jit(solution)/shard_map/all_gather | solution.py:111
  176.3 308.9 %reduce-scatter.5.cloned.1.call-start = ((), (), s32[]{:S(2)}) async-start(), calls=%async_computation.10 | async-start | bytes 1179648 | tf_op jit(solution)/shard_map/reduce_scatter | solution.py:113
  253.2 3.8 collective-permute-start
  254.2 4.4 collective-permute-start.1
  256.9 5.6 collective-permute-start.2
  258.6 4.4 collective-permute-start.3
  262.5 5.6 collective-permute-start.4
  262.9 5.4 collective-permute-start.5
  268.2 5.6 collective-permute-start.6
  273.8 133.2 %copy-start.8 = (s32[2,16,4]{1,2,0:T(4,128)S(1)}, s32[2,16,4]{1,2,0:T(4,128)}, u32[]{:S(2)}) copy-start(s32[2,16,4]{1,2,0:T(4,128)} %param.27) | copy-start | bytes 1540
  273.8 142.8 %copy-start.9 = (bf16[4,128]{1,0:T(4,128)(2,1)S(1)}, bf16[4,128]{1,0:T(4,128)(2,1)}, u32[]{:S(2)}) copy-start(bf16[4,128]{1,0:T(4,128)(2,1)} %param.23) | copy-start | bytes 3076
  410.5 94.4 %all-to-all-start = ((s32[32,1,8]{2,1,0:T(1,128)}), s32[32,1,8]{2,1,0:T(1,128)S(1)}, u32[]{:S(2)}, u32[]{:S(2)}) async-start(s32[32,1,8]{2,1,0:T(1,128)} %bitcast.21), calls=%async_computation.2 | async-start | bytes 32768 | tf_op jit(solution)/shard_map/all_to_all | solution.py:145
  488.8 2.5 copy-start.2
  504.9 55.5 %all-to-all-start.1 = ((bf16[32,8,32,128]{3,2,1,0:T(8,128)(2,1)}), bf16[32,8,32,128]{3,2,1,0:T(8,128)(2,1)S(1)}, u32[]{:S(2)}, u32[]{:S(2)}) async-start(bf16[32,8,32,128]{3,2,1,0:T(8,128)(2,1)} %bitcast.24), calls=%async_computation.3 | async-start | bytes 4194304 | tf_op jit(solution)/shard_map/all_to_all | solution.py:150
  512.0 11.8 %copy-start.1 = (s32[256]{0:T(256)S(1)}, s32[256]{0:T(256)}, u32[]{:S(2)}) copy-start(s32[256]{0:T(256)} %param.25) | copy-start | bytes 3076
  569.1 16.4 %all-to-all-start.2 = ((bf16[32,2,128]{2,1,0:T(2,128)(2,1)}), bf16[32,2,128]{2,1,0:T(2,128)(2,1)S(1)}, u32[]{:S(2)}, u32[]{:S(2)}) async-start(bf16[32,2,128]{2,1,0:T(2,128)(2,1)} %reshape.374), calls=%async_computation.4 | async-start | bytes 32768 | tf_op jit(solution)/shard_map/all_to_all | solution.py:21
Sparse Core Ops, SparseCore 0:
  9.8 29.9 all-gather.5
  42.4 71.4 all-gather.7
  175.3 74.5 reduce-scatter.2
  252.3 72.4 all-gather.9
  327.2 73.8 all-gather.11
  407.1 35.2 reduce-scatter.4
